TPU v7x, 32 devices: a whole 2x2x4 slice. The times are simulated.
32 devices in a mesh: parts: 2 (over x), chan: 8 (over z, y), samp: 2 (over core).
Axes of the slice: x: 2, y: 2, z: 4, core: 2. Of those that a mesh axis runs over, the one named last changes fastest.
Arguments:
- images: bfloat16 [512, 256, 784], P(('parts', 'samp'), 'chan'), parts along dimension 0, may hold values from -6 to 6
- out_grads: bfloat16 [512, 256, 196], P(('parts', 'samp'), 'chan'), parts along dimension 0, may hold values from -6 to 6
- in_signs: int32 [256, 288], P('chan'), may hold values from 0 to 1
- out_signs: int32 [256, 32], P('chan'), may hold values from 0 to 1
Outputs:
- sketch_rows: float32 [2, 256, 1024], P('samp', ('parts', 'chan')), parts along dimension 1
- r_factor: float32 [2048, 1024], P(('parts', 'chan')), parts along dimension 0
There are 2 independent parts, one for each index of `parts`. A program takes and returns all parts, laid end to end along the dimension named above; an argument that names none is the same for every part. Nothing has to cross between parts.
All inputs are finite; a program needn't handle non-finite values.
Results may differ from a plain program's by a relative error of at most 0.0003.
Values sent between devices are 32-bit elements; how exact they have to be, the bound alone decides.
No kernel may reach another device: no remote copies, remote signals or barrier semaphores. Data moves between devices by JAX's collectives and lax.ppermute only.
A program may use at most 128 MiB of HBM per device.

v0:
```python
import math
import jax
import jax.numpy as jnp
from jax import lax
from jax.sharding import PartitionSpec as P

C = 256


def project(images, out_grads, in_signs, out_signs):
    samples, channels, cells = images.shape
    side_in = math.isqrt(cells)
    side_out = side_in // 2
    picture = images.reshape(samples, channels, side_in, side_in)
    padded = jnp.pad(picture, ((0, 0), (0, 0), (1, 1), (1, 1)))
    tap_list = []
    for row_tap in range(3):
        for col_tap in range(3):
            tap_list.append(
                padded[
                    :,
                    :,
                    row_tap : row_tap + 2 * side_out - 1 : 2,
                    col_tap : col_tap + 2 * side_out - 1 : 2,
                ]
            )
    patches = jnp.stack(tap_list, axis=2).reshape(samples, channels, 9, side_out * side_out)
    width_in = in_signs.shape[1] // 9
    in_matrix = (2 * in_signs - 1).astype(jnp.bfloat16).reshape(channels, 9, width_in)
    out_matrix = (2 * out_signs - 1).astype(jnp.bfloat16)
    in_part = jnp.einsum("nctp,ctj->njp", patches, in_matrix, preferred_element_type=jnp.float32)
    out_part = jnp.einsum("ncp,cl->nlp", out_grads, out_matrix, preferred_element_type=jnp.float32)
    return (in_part, out_part)


def sketch(in_sum, out_sum, total_channels):
    in_feat = in_sum / math.sqrt(9 * total_channels)
    out_feat = out_sum / math.sqrt(total_channels)
    cells = in_sum.shape[2]
    outer = jnp.einsum(
        "nlp,njp->nlj", out_feat, in_feat, precision=lax.Precision.HIGHEST
    ) / math.sqrt(cells)
    return outer.reshape(outer.shape[0], -1)


def local(images, out_grads, in_signs, out_signs):
    samples = images.shape[0]
    in_part, out_part = project(images, out_grads, in_signs, out_signs)
    chan_count = lax.axis_size("chan")
    local_rows = samples // chan_count
    in_sum, out_sum = lax.psum((in_part, out_part), "chan")
    every = sketch(in_sum, out_sum, C)
    own = lax.dynamic_slice_in_dim(every, lax.axis_index("chan") * local_rows, local_rows, 0)
    batch_total = samples * lax.axis_size("samp")
    width = every.shape[1]
    identity_mat = jnp.eye(width, dtype=jnp.float32)
    gram_part = jnp.einsum("nk,nm->km", every, every, precision=lax.Precision.HIGHEST) / batch_total
    factor = jnp.linalg.cholesky(lax.psum(gram_part, "samp") + identity_mat).T
    rows_here = width // chan_count
    r_rows = lax.dynamic_slice_in_dim(factor, lax.axis_index("chan") * rows_here, rows_here, 0)
    return (own[None], r_rows)


def solution(mesh):
    in_specs = (
        P(("parts", "samp"), "chan", None),
        P(("parts", "samp"), "chan", None),
        P("chan", None),
        P("chan", None),
    )
    out_specs = (P("samp", ("parts", "chan"), None), P(("parts", "chan"), None))
    return jax.shard_map(local, mesh=mesh, in_specs=in_specs, out_specs=out_specs, check_vma=False)
```

profile of v0, /device:TPU:0, one launch (start us, length us, event | category | flops | bytes accessed | tf_op | source)
XLA Modules:
  0.0 630.9 jit_solution(10612608494008498298)
XLA Ops:
  11.7 5.5 pad_slice_fusion
  30.4 4.8 copy.40
  71.6 12.2 %convolution_bitcast_fusion = f32[128,32,196]{2,1,0:T(8,128)} fusion(bf16[32,9,32,1]{0,2,1,3:T(8,128)(2,1)S(1)} %bitcast.86, bf16[128,32,9,196]{3,1,2,0:T(8,128)(2,1)} %constant_dynamic-update-slice_fusion), kind=kOutput, calls=%fused_computation.16 | convolution fusion | flops 462422016 | bytes 17680384 | tf_op jit(solution)/shard_map/nctp,ctj->njp/dot_general | solution.py:31
  87.0 273.4 %all-reduce.8.cloned.1.call-done = (f32[128,32,196]{2,1,0:T(8,128)}, f32[128,32,196]{2,1,0:T(8,128)}) async-done(((f32[128,32,196]{2,1,0:T(8,128)}, f32[128,32,196]{2,1,0:T(8,128)}), (f32[128,32,196]{2,1,0:T(8,128)}, f32[128,32,196]{2,1,0:T(8,128)})) %all-reduce.8.cloned.1.call-update) | async-done | bytes 6422544 | tf_op jit(solution)/shard_map/psum | solution.py:51
  360.5 7.8 %fusion.6 = f32[128,32,32]{2,1,0:T(8,128)S(1)} fusion(f32[128,32,196]{2,1,0:T(8,128)} %get-tuple-element.10, f32[128,32,196]{2,1,0:T(8,128)} %get-tuple-element.11), kind=kOutput, calls=%fused_computation.21 | convolution fusion | flops 310018048 | bytes 6946816 | tf_op jit(solution)/shard_map/nlp,njp->nlj/dot_general | solution.py:40
  369.5 5.0 convolution_multiply_fusion
  375.6 26.6 %all-reduce.6.cloned.1.call-done = f32[1024,1024]{0,1:T(8,128)} async-done(((f32[1024,1024]{0,1:T(8,128)}), f32[1024,1024]{0,1:T(8,128)}) %all-reduce.6.cloned.1.call-update) | async-done | bytes 4194320 | tf_op jit(solution)/shard_map/psum | solution.py:58
  402.2 4.8 convert_add_fusion
  407.0 5.5 copy.49
  418.9 11.7 %cholesky.223 = f32[128,128]{1,0:T(8,128)S(1)} custom-call(f32[128,128]{1,0:T(8,128)S(1)} %cholesky.580), custom_call_target="Cholesky" | custom-call | tf_op jit(solution)/shard_map/jit(cholesky)/cholesky | solution.py:58
  433.1 9.8 %custom-call.59 = f32[1,128,128]{1,2,0:T(8,128)S(1)} custom-call(f32[1,128,128]{2,1,0:T(8,128)S(1)} %get-tuple-element.42), custom_call_target="InvertDiagBlocksLowerTriangular" | custom-call | tf_op jit(solution)/shard_map/jit(cholesky)/cholesky | solution.py:58
  446.9 11.9 %cholesky.244 = f32[128,128]{1,0:T(8,128)S(1)} custom-call(f32[128,128]{1,0:T(8,128)S(1)} %cholesky.584), custom_call_target="Cholesky" | custom-call | tf_op jit(solution)/shard_map/jit(cholesky)/cholesky | solution.py:58
  459.4 9.8 %custom-call.60 = f32[1,128,128]{1,2,0:T(8,128)S(1)} custom-call(f32[1,128,128]{2,1,0:T(8,128)S(1)} %get-tuple-element.39), custom_call_target="InvertDiagBlocksLowerTriangular" | custom-call | tf_op jit(solution)/shard_map/jit(cholesky)/cholesky | solution.py:58
  472.6 11.7 %cholesky.468 = f32[128,128]{1,0:T(8,128)S(1)} custom-call(f32[128,128]{1,0:T(8,128)S(1)} %cholesky.589), custom_call_target="Cholesky" | custom-call | tf_op jit(solution)/shard_map/jit(cholesky)/cholesky | solution.py:58
  485.6 9.8 %custom-call.61 = f32[1,128,128]{1,2,0:T(8,128)S(1)} custom-call(f32[1,128,128]{2,1,0:T(8,128)S(1)} %get-tuple-element.36), custom_call_target="InvertDiagBlocksLowerTriangular" | custom-call | tf_op jit(solution)/shard_map/jit(cholesky)/cholesky | solution.py:58
  498.9 12.1 %cholesky.487 = f32[128,128]{1,0:T(8,128)S(1)} custom-call(f32[128,128]{1,0:T(8,128)S(1)} %cholesky.594), custom_call_target="Cholesky" | custom-call | tf_op jit(solution)/shard_map/jit(cholesky)/cholesky | solution.py:58
  512.3 9.8 %custom-call.62 = f32[1,128,128]{1,2,0:T(8,128)S(1)} custom-call(f32[1,128,128]{2,1,0:T(8,128)S(1)} %get-tuple-element.33), custom_call_target="InvertDiagBlocksLowerTriangular" | custom-call | tf_op jit(solution)/shard_map/jit(cholesky)/cholesky | solution.py:58
  525.6 11.7 %cholesky.506 = f32[128,128]{1,0:T(8,128)S(1)} custom-call(f32[128,128]{1,0:T(8,128)S(1)} %cholesky.599), custom_call_target="Cholesky" | custom-call | tf_op jit(solution)/shard_map/jit(cholesky)/cholesky | solution.py:58
  538.6 9.9 %custom-call.63 = f32[1,128,128]{1,2,0:T(8,128)S(1)} custom-call(f32[1,128,128]{2,1,0:T(8,128)S(1)} %get-tuple-element.30), custom_call_target="InvertDiagBlocksLowerTriangular" | custom-call | tf_op jit(solution)/shard_map/jit(cholesky)/cholesky | solution.py:58
  551.8 11.7 %cholesky.526 = f32[128,128]{1,0:T(8,128)S(1)} custom-call(f32[128,128]{1,0:T(8,128)S(1)} %cholesky.604), custom_call_target="Cholesky" | custom-call | tf_op jit(solution)/shard_map/jit(cholesky)/cholesky | solution.py:58
  564.8 9.8 %custom-call.64 = f32[1,128,128]{1,2,0:T(8,128)S(1)} custom-call(f32[1,128,128]{2,1,0:T(8,128)S(1)} %get-tuple-element.27), custom_call_target="InvertDiagBlocksLowerTriangular" | custom-call | tf_op jit(solution)/shard_map/jit(cholesky)/cholesky | solution.py:58
  577.6 11.9 %cholesky.546 = f32[128,128]{1,0:T(8,128)S(1)} custom-call(f32[128,128]{1,0:T(8,128)S(1)} %cholesky.609), custom_call_target="Cholesky" | custom-call | tf_op jit(solution)/shard_map/jit(cholesky)/cholesky | solution.py:58
  590.8 9.8 %custom-call.65 = f32[1,128,128]{1,2,0:T(8,128)S(1)} custom-call(f32[1,128,128]{2,1,0:T(8,128)S(1)} %get-tuple-element.24), custom_call_target="InvertDiagBlocksLowerTriangular" | custom-call | tf_op jit(solution)/shard_map/jit(cholesky)/cholesky | solution.py:58
  603.2 11.7 %cholesky.564 = f32[128,128]{1,0:T(8,128)S(1)} custom-call(f32[128,128]{1,0:T(8,128)S(1)} %convolution_subtract_fusion.6), custom_call_target="Cholesky" | custom-call | tf_op jit(solution)/shard_map/jit(cholesky)/cholesky | solution.py:58
  (99 shorter events, 102.7 us)
Async XLA Ops:
  7.2 353.3 %all-reduce.8.cloned.1.call-start = ((), (), s32[]{:S(2)}) async-start(), calls=%async_computation.1 | async-start | bytes 16777216 | tf_op jit(solution)/shard_map/psum | solution.py:51
  22.3 4.8 copy-start.12
  27.1 8.2 %copy-start.11 = (bf16[128,32,14,14]{0,1,3,2:T(8,128)(2,1)S(1)}, bf16[128,32,14,14]{0,1,3,2:T(8,128)(2,1)}, u32[]{:S(2)}) copy-start(bf16[128,32,14,14]{0,1,3,2:T(8,128)(2,1)} %get-tuple-element.16) | copy-start | bytes 4816900
  30.4 8.2 %copy-start.10 = (bf16[128,32,14,14]{0,1,3,2:T(8,128)(2,1)S(1)}, bf16[128,32,14,14]{0,1,3,2:T(8,128)(2,1)}, u32[]{:S(2)}) copy-start(bf16[128,32,14,14]{0,1,3,2:T(8,128)(2,1)} %get-tuple-element.17) | copy-start | bytes 4816900
  38.6 8.2 %copy-start.9 = (bf16[128,32,14,14]{0,1,3,2:T(8,128)(2,1)S(1)}, bf16[128,32,14,14]{0,1,3,2:T(8,128)(2,1)}, u32[]{:S(2)}) copy-start(bf16[128,32,14,14]{0,1,3,2:T(8,128)(2,1)} %get-tuple-element.19) | copy-start | bytes 4816900
  42.0 8.2 %copy-start.8 = (bf16[128,32,14,14]{0,1,3,2:T(8,128)(2,1)S(1)}, bf16[128,32,14,14]{0,1,3,2:T(8,128)(2,1)}, u32[]{:S(2)}) copy-start(bf16[128,32,14,14]{0,1,3,2:T(8,128)(2,1)} %get-tuple-element.12) | copy-start | bytes 4816900
  46.9 6.7 %copy-start.13 = (s32[32,288]{1,0:T(8,128)S(1)}, s32[32,288]{1,0:T(8,128)}, u32[]{:S(2)}) copy-start(s32[32,288]{1,0:T(8,128)} %param.6) | copy-start | bytes 110596
  57.3 3.4 copy-start.7
  57.4 4.9 copy-start.6
  60.8 3.1 copy-start.5
  62.3 3.1 copy-start.4
  63.8 3.1 copy-start.3
  65.4 3.1 copy-start.1
  66.9 3.1 copy-start.2
  71.6 12.2 %copy-start.14 = (s32[32,32]{1,0:T(8,128)S(1)}, s32[32,32]{1,0:T(8,128)}, u32[]{:S(2)}) copy-start(s32[32,32]{1,0:T(8,128)} %param.7) | copy-start | bytes 12292
  86.5 315.6 %all-reduce.6.cloned.1.call-start = ((), (), s32[]{:S(2)}) async-start(), calls=%async_computation | async-start | bytes 8388608 | tf_op jit(solution)/shard_map/psum | solution.py:58
  416.9 1.9 copy-start
Sparse Core Ops, SparseCore 0:
  86.7 273.7 all-reduce.7
  374.7 27.4 all-reduce.5
where the time goes:
time: 641 us; the launch traced here: 631 us
  waiting for transfers between devices  300 us (47%)
  other arithmetic  183 us (29%)
  local copies, waits for them, and re-layouts  77.6 us (12%)
  matrix products  50.8 us (8%)
  between operations  19.4 us (3%)
    psum x1, waiting for transfers between devices, local(): in_sum, out_sum = lax.psum((in_part, out_part), 'chan')  273 us
    another operation x30, other arithmetic, local(): factor = jnp.linalg.cholesky(lax.psum(gram_part, 'samp') + identity_mat).T  172 us
    another operation x10, local copies, waits for them, and re-layouts, project(): jnp.stack(tap_list, axis=2)  36.4 us
    psum x1, waiting for transfers between devices, local(): factor = jnp.linalg.cholesky(lax.psum(gram_part, 'samp') + identity_mat).T  26.6 us
    unnamed x41, local copies, waits for them, and re-layouts  25.2 us
    another operation x14, matrix products, local(): factor = jnp.linalg.cholesky(lax.psum(gram_part, 'samp') + identity_mat).T  23.1 us
  transfers between devices with their start and end apart: 2, of which 2 were waited for; matrix products, arithmetic and copies ran while one was open for 0% of the time, Pallas kernels for 0%

commit v1 on v0

--- a/solution.py
+++ b/solution.py
@@ -55,7 +55,9 @@
     width = every.shape[1]
     identity_mat = jnp.eye(width, dtype=jnp.float32)
     gram_part = jnp.einsum("nk,nm->km", every, every, precision=lax.Precision.HIGHEST) / batch_total
-    factor = jnp.linalg.cholesky(lax.psum(gram_part, "samp") + identity_mat).T
+    factor = jnp.linalg.cholesky(
+        jnp.sum(lax.all_gather(gram_part, "samp"), axis=0) + identity_mat
+    ).T
     rows_here = width // chan_count
     r_rows = lax.dynamic_slice_in_dim(factor, lax.axis_index("chan") * rows_here, rows_here, 0)
     return (own[None], r_rows)

time: 641 us -> 635 us (level)
  waiting for transfers between devices: 300 us -> 291 us
    psum x1 -> x0, waiting for transfers between devices: 26.6 us -> none  [local(): factor = jnp.linalg.cholesky(lax.psum(gram_part, 'samp') + identity_mat).T]
    all_gather x0 -> x1, waiting for transfers between devices: none -> 18 us  [local(): lax.all_gather(gram_part, 'samp')]
    reduce_sum x0 -> x1, other arithmetic: none -> 6.68 us  [local(): jnp.sum(lax.all_gather(gram_part, 'samp'), axis=0) + identity_mat]
where the time goes in v1:
time: 635 us; the launch traced here: 624 us
  waiting for transfers between devices  291 us (46%)
  other arithmetic  185 us (29%)
  local copies, waits for them, and re-layouts  77.6 us (12%)
  matrix products  50.7 us (8%)
  between operations  19.4 us (3%)
    psum x1, waiting for transfers between devices, local(): in_sum, out_sum = lax.psum((in_part, out_part), 'chan')  273 us
    another operation x30, other arithmetic, local(): jnp.linalg.cholesky(jnp.sum(lax.all_gather(gram_part, 'samp'), axis=0) +...  172 us
    another operation x10, local copies, waits for them, and re-layouts, project(): jnp.stack(tap_list, axis=2)  36.4 us
    unnamed x41, local copies, waits for them, and re-layouts  25.2 us
    another operation x14, matrix products, local(): jnp.linalg.cholesky(jnp.sum(lax.all_gather(gram_part, 'samp'), axis=0) +...  23.1 us
    all_gather x1, waiting for transfers between devices, local(): lax.all_gather(gram_part, 'samp')  18 us
  transfers between devices with their start and end apart: 2, of which 2 were waited for; matrix products, arithmetic and copies ran while one was open for 0% of the time, Pallas kernels for 0%

profile of v1, /device:TPU:0, one launch (start us, length us, event | category | flops | bytes accessed | tf_op | source)
XLA Modules:
  0.0 624.2 jit_solution(8908478942788284648)
XLA Ops:
  11.7 5.5 pad_slice_fusion
  30.4 4.8 copy.54
  71.6 12.2 %convolution_bitcast_fusion = f32[128,32,196]{2,1,0:T(8,128)} fusion(bf16[32,9,32,1]{0,2,1,3:T(8,128)(2,1)S(1)} %bitcast.90, bf16[128,32,9,196]{3,1,2,0:T(8,128)(2,1)} %constant_dynamic-update-slice_fusion), kind=kOutput, calls=%fused_computation.17 | convolution fusion | flops 462422016 | bytes 17680384 | tf_op jit(solution)/shard_map/nctp,ctj->njp/dot_general | solution.py:31
  87.0 273.4 %all-reduce.5.cloned.1.call-done = (f32[128,32,196]{2,1,0:T(8,128)}, f32[128,32,196]{2,1,0:T(8,128)}) async-done(((f32[128,32,196]{2,1,0:T(8,128)}, f32[128,32,196]{2,1,0:T(8,128)}), (f32[128,32,196]{2,1,0:T(8,128)}, f32[128,32,196]{2,1,0:T(8,128)})) %all-reduce.5.cloned.1.call-update) | async-done | bytes 6422544 | tf_op jit(solution)/shard_map/psum | solution.py:51
  360.5 7.8 %fusion.7 = f32[128,32,32]{2,1,0:T(8,128)S(1)} fusion(f32[128,32,196]{2,1,0:T(8,128)} %get-tuple-element.12, f32[128,32,196]{2,1,0:T(8,128)} %get-tuple-element.13), kind=kOutput, calls=%fused_computation.22 | convolution fusion | flops 310018048 | bytes 6946816 | tf_op jit(solution)/shard_map/nlp,njp->nlj/dot_general | solution.py:40
  369.5 5.0 convolution_multiply_fusion
  375.5 18.0 %all-gather.3.cloned.1.call-done = f32[2048,1024]{1,0:T(8,128)} async-done(((f32[1024,1024]{1,0:T(8,128)}), f32[2048,1024]{1,0:T(8,128)}) %all-gather.3.cloned.1.call-update) | async-done | bytes 8388624 | tf_op jit(solution)/shard_map/all_gather | solution.py:59
  393.5 6.7 %reduce_sum.11 = f32[1024,1024]{1,0:T(8,128)} reduce(f32[2,1024,1024]{2,1,0:T(8,128)} %bitcast.80, f32[]{:T(128)} %constant.293.clone.1), dimensions={0}, to_apply=%region_2.3 | reduce | flops 1048576 | bytes 12582916 | tf_op jit(solution)/shard_map/reduce_sum | solution.py:59
  400.2 5.5 copy.62
  412.1 11.7 %cholesky.223 = f32[128,128]{1,0:T(8,128)S(1)} custom-call(f32[128,128]{1,0:T(8,128)S(1)} %cholesky.580), custom_call_target="Cholesky" | custom-call | tf_op jit(solution)/shard_map/jit(cholesky)/cholesky | solution.py:58
  426.4 9.8 %custom-call.59 = f32[1,128,128]{1,2,0:T(8,128)S(1)} custom-call(f32[1,128,128]{2,1,0:T(8,128)S(1)} %get-tuple-element.44), custom_call_target="InvertDiagBlocksLowerTriangular" | custom-call | tf_op jit(solution)/shard_map/jit(cholesky)/cholesky | solution.py:58
  440.1 11.9 %cholesky.244 = f32[128,128]{1,0:T(8,128)S(1)} custom-call(f32[128,128]{1,0:T(8,128)S(1)} %cholesky.584), custom_call_target="Cholesky" | custom-call | tf_op jit(solution)/shard_map/jit(cholesky)/cholesky | solution.py:58
  452.6 9.8 %custom-call.60 = f32[1,128,128]{1,2,0:T(8,128)S(1)} custom-call(f32[1,128,128]{2,1,0:T(8,128)S(1)} %get-tuple-element.41), custom_call_target="InvertDiagBlocksLowerTriangular" | custom-call | tf_op jit(solution)/shard_map/jit(cholesky)/cholesky | solution.py:58
  465.8 11.7 %cholesky.468 = f32[128,128]{1,0:T(8,128)S(1)} custom-call(f32[128,128]{1,0:T(8,128)S(1)} %cholesky.589), custom_call_target="Cholesky" | custom-call | tf_op jit(solution)/shard_map/jit(cholesky)/cholesky | solution.py:58
  478.8 9.8 %custom-call.61 = f32[1,128,128]{1,2,0:T(8,128)S(1)} custom-call(f32[1,128,128]{2,1,0:T(8,128)S(1)} %get-tuple-element.38), custom_call_target="InvertDiagBlocksLowerTriangular" | custom-call | tf_op jit(solution)/shard_map/jit(cholesky)/cholesky | solution.py:58
  492.1 12.1 %cholesky.487 = f32[128,128]{1,0:T(8,128)S(1)} custom-call(f32[128,128]{1,0:T(8,128)S(1)} %cholesky.594), custom_call_target="Cholesky" | custom-call | tf_op jit(solution)/shard_map/jit(cholesky)/cholesky | solution.py:58
  505.5 9.8 %custom-call.62 = f32[1,128,128]{1,2,0:T(8,128)S(1)} custom-call(f32[1,128,128]{2,1,0:T(8,128)S(1)} %get-tuple-element.35), custom_call_target="InvertDiagBlocksLowerTriangular" | custom-call | tf_op jit(solution)/shard_map/jit(cholesky)/cholesky | solution.py:58
  518.8 11.7 %cholesky.506 = f32[128,128]{1,0:T(8,128)S(1)} custom-call(f32[128,128]{1,0:T(8,128)S(1)} %cholesky.599), custom_call_target="Cholesky" | custom-call | tf_op jit(solution)/shard_map/jit(cholesky)/cholesky | solution.py:58
  531.8 10.0 %custom-call.63 = f32[1,128,128]{1,2,0:T(8,128)S(1)} custom-call(f32[1,128,128]{2,1,0:T(8,128)S(1)} %get-tuple-element.32), custom_call_target="InvertDiagBlocksLowerTriangular" | custom-call | tf_op jit(solution)/shard_map/jit(cholesky)/cholesky | solution.py:58
  545.1 11.7 %cholesky.526 = f32[128,128]{1,0:T(8,128)S(1)} custom-call(f32[128,128]{1,0:T(8,128)S(1)} %cholesky.604), custom_call_target="Cholesky" | custom-call | tf_op jit(solution)/shard_map/jit(cholesky)/cholesky | solution.py:58
  558.1 9.8 %custom-call.64 = f32[1,128,128]{1,2,0:T(8,128)S(1)} custom-call(f32[1,128,128]{2,1,0:T(8,128)S(1)} %get-tuple-element.29), custom_call_target="InvertDiagBlocksLowerTriangular" | custom-call | tf_op jit(solution)/shard_map/jit(cholesky)/cholesky | solution.py:58
  570.9 11.9 %cholesky.546 = f32[128,128]{1,0:T(8,128)S(1)} custom-call(f32[128,128]{1,0:T(8,128)S(1)} %cholesky.609), custom_call_target="Cholesky" | custom-call | tf_op jit(solution)/shard_map/jit(cholesky)/cholesky | solution.py:58
  584.0 9.8 %custom-call.65 = f32[1,128,128]{1,2,0:T(8,128)S(1)} custom-call(f32[1,128,128]{2,1,0:T(8,128)S(1)} %get-tuple-element.26), custom_call_target="InvertDiagBlocksLowerTriangular" | custom-call | tf_op jit(solution)/shard_map/jit(cholesky)/cholesky | solution.py:58
  596.4 11.7 %cholesky.564 = f32[128,128]{1,0:T(8,128)S(1)} custom-call(f32[128,128]{1,0:T(8,128)S(1)} %convolution_subtract_fusion.6), custom_call_target="Cholesky" | custom-call | tf_op jit(solution)/shard_map/jit(cholesky)/cholesky | solution.py:58
  (99 shorter events, 102.7 us)
Async XLA Ops:
  7.2 353.3 %all-reduce.5.cloned.1.call-start = ((), (), s32[]{:S(2)}) async-start(), calls=%async_computation.1 | async-start | bytes 16777216 | tf_op jit(solution)/shard_map/psum | solution.py:51
  22.3 4.8 copy-start.12
  27.1 8.2 %copy-start.11 = (bf16[128,32,14,14]{0,1,3,2:T(8,128)(2,1)S(1)}, bf16[128,32,14,14]{0,1,3,2:T(8,128)(2,1)}, u32[]{:S(2)}) copy-start(bf16[128,32,14,14]{0,1,3,2:T(8,128)(2,1)} %get-tuple-element.18) | copy-start | bytes 4816900
  30.4 8.2 %copy-start.10 = (bf16[128,32,14,14]{0,1,3,2:T(8,128)(2,1)S(1)}, bf16[128,32,14,14]{0,1,3,2:T(8,128)(2,1)}, u32[]{:S(2)}) copy-start(bf16[128,32,14,14]{0,1,3,2:T(8,128)(2,1)} %get-tuple-element.19) | copy-start | bytes 4816900
  38.6 8.2 %copy-start.9 = (bf16[128,32,14,14]{0,1,3,2:T(8,128)(2,1)S(1)}, bf16[128,32,14,14]{0,1,3,2:T(8,128)(2,1)}, u32[]{:S(2)}) copy-start(bf16[128,32,14,14]{0,1,3,2:T(8,128)(2,1)} %get-tuple-element.21) | copy-start | bytes 4816900
  42.0 8.2 %copy-start.8 = (bf16[128,32,14,14]{0,1,3,2:T(8,128)(2,1)S(1)}, bf16[128,32,14,14]{0,1,3,2:T(8,128)(2,1)}, u32[]{:S(2)}) copy-start(bf16[128,32,14,14]{0,1,3,2:T(8,128)(2,1)} %get-tuple-element.14) | copy-start | bytes 4816900
  46.9 6.7 %copy-start.13 = (s32[32,288]{1,0:T(8,128)S(1)}, s32[32,288]{1,0:T(8,128)}, u32[]{:S(2)}) copy-start(s32[32,288]{1,0:T(8,128)} %param.6) | copy-start | bytes 110596
  57.3 3.4 copy-start.7
  57.4 4.9 copy-start.6
  60.8 3.1 copy-start.5
  62.3 3.1 copy-start.4
  63.8 3.1 copy-start.3
  65.4 3.1 copy-start.1
  66.9 3.1 copy-start.2
  71.6 12.2 %copy-start.14 = (s32[32,32]{1,0:T(8,128)S(1)}, s32[32,32]{1,0:T(8,128)}, u32[]{:S(2)}) copy-start(s32[32,32]{1,0:T(8,128)} %param.7) | copy-start | bytes 12292
  86.5 307.0 %all-gather.3.cloned.1.call-start = ((), (), s32[]{:S(2)}) async-start(), calls=%async_computation | async-start | bytes 12582912 | tf_op jit(solution)/shard_map/all_gather | solution.py:59
  410.2 1.9 copy-start
Sparse Core Ops, SparseCore 0:
  86.7 273.7 all-reduce.4
  374.6 18.8 all-gather.2
